TPU v7x, 32 devices: a whole 2x2x4 slice. The times are simulated.
32 devices in a mesh: depth: 8 (over z, y), rows: 4 (over x, core).
Axes of the slice: x: 2, y: 2, z: 4, core: 2. Of those that a mesh axis runs over, the one named last changes fastest.
Arguments:
- density_raw: bfloat16 [256, 64, 1024], P('depth', 'rows'), may hold values from -6 to 6
- colour_raw: bfloat16 [3, 256, 64, 1024], P(None, 'depth', 'rows'), may hold values from -6 to 6
- target: float32 [3, 64, 1024], P(None, 'rows'), may hold values from 0 to 1
- slab_rank: int32 [8], replicated, may hold values from 0 to 7, each once
Outputs:
- grad_density: float32 [256, 64, 1024], P('depth', 'rows')
- grad_colour: float32 [3, 256, 64, 1024], P(None, 'depth', 'rows')
Inputs may be any that keep to these rules, and one draw needn't show every extreme that they name: slab_rank is a permutation: every slab has its own position along the rays.
All inputs are finite; a program needn't handle non-finite values.
Results may differ from a plain program's by a relative error of at most 0.0003.
Values may be sent and summed in bfloat16 or wider, within the bound.
No kernel may reach another device: no remote copies, remote signals or barrier semaphores. Data moves between devices by JAX's collectives and lax.ppermute only.
A program may use at most 128 MiB of HBM per device.

v0:
```python
import jax
import jax.numpy as jnp
from jax import lax
from jax.sharding import PartitionSpec as P

optical_depth = 2.5
smooth_weight = 0.05


def extended(value, sides, width):
    for axis, dim in sides:
        peers, length = (lax.axis_size(axis), value.shape[dim])
        up = [(i, (i + 1) % peers) for i in range(peers - 1)]
        down = [(j, i) for i, j in up]
        last = lax.slice_in_dim(value, length - width, length, axis=dim)
        initial = lax.slice_in_dim(value, 0, width, axis=dim)
        before = lax.ppermute(last, axis, up)
        after = lax.ppermute(initial, axis, down)
        value = jnp.concatenate([before, value, after], axis=dim)
    return value


def along_rays(matrix, values):
    shape = values.shape
    flat = values.reshape(shape[0], shape[1], -1)
    mixed = jnp.einsum("ij,cjp->cip", matrix, flat, precision=lax.Precision.HIGHEST)
    return mixed.reshape(shape)


def triangles(count):
    index = jnp.arange(count, dtype=jnp.int32)
    before = (index[None, :] < index[:, None]).astype(jnp.float32)
    after = (index[None, :] > index[:, None]).astype(jnp.float32)
    return (before, after)


def slab_terms(density, colour_raw, step_depth):
    dense = density.astype(jnp.float32)
    colour = jax.nn.sigmoid(colour_raw.astype(jnp.float32))
    depth_term = step_depth * jax.nn.softplus(dense)
    opacity = -jnp.expm1(-depth_term)
    kept = jnp.exp(-depth_term)
    before, after = triangles(dense.shape[0])
    front_light = jnp.exp(-along_rays(before, depth_term[None]))[0]
    through = front_light * kept
    passing = jnp.exp(-jnp.sum(depth_term, axis=0))
    weighted = front_light[None] * opacity[None] * colour
    behind_local = along_rays(after, weighted) / through[None]
    after_light = passing[None] / through
    partial_value = jnp.concatenate([jnp.sum(weighted, axis=1), passing[None]], axis=0)
    return (partial_value, (dense, colour, opacity, behind_local, after_light, front_light))


def slab_gradients(saved, scaled_residual, scaled_behind, slices_total):
    dense, colour, opacity, behind_local, after_light, front_light = saved
    lit = front_light * opacity
    grad_colour = slices_total * scaled_residual[:, None] * lit[None] * colour * (1.0 - colour)
    inner = (
        jnp.sum(scaled_residual[:, None] * (colour - behind_local), axis=0)
        - after_light * scaled_behind[None]
    )
    grad_density = optical_depth * front_light * (1.0 - opacity) * jax.nn.sigmoid(dense) * inner
    return (grad_density, grad_colour)


def composite(partials, slab_rank, target_piece):
    count = partials.shape[1]
    one_hot = (slab_rank[:, None] == jnp.arange(count, dtype=jnp.int32)[None]).astype(
        partials.dtype
    )
    ordered = jnp.einsum("sk,csl->ckl", one_hot, partials, precision=lax.Precision.HIGHEST)
    emitted, kept = (ordered[:3], ordered[3:])
    before, after = triangles(count)
    front = jnp.exp(along_rays(before, jnp.log(kept)))
    weighted = front * emitted
    behind = along_rays(after, weighted) / (front * kept)
    residual = jnp.sum(weighted, axis=1) - target_piece
    scaled_residual = front * residual[:, None]
    scaled_behind = front * jnp.sum(residual[:, None] * behind, axis=0, keepdims=True)
    stacked = jnp.concatenate([scaled_residual, scaled_behind], axis=0)
    return jnp.einsum("sk,ckl->csl", one_hot, stacked, precision=lax.Precision.HIGHEST)


def smooth_rims(density_raw, slices_dev, rows_dev):
    padded = extended(density_raw, (("depth", 0), ("rows", 1)), 1).astype(jnp.float32)
    centre = padded[1:-1, 1:-1]
    slice_index = lax.axis_index("depth") * slices_dev + jnp.arange(slices_dev, dtype=jnp.int32)
    row_index = lax.axis_index("rows") * rows_dev + jnp.arange(rows_dev, dtype=jnp.int32)
    last_slice = slices_dev * lax.axis_size("depth") - 1
    last_row = rows_dev * lax.axis_size("rows") - 1
    below = jnp.where((slice_index > 0)[:, None, None], centre - padded[:-2, 1:-1], 0.0)
    above = jnp.where((slice_index < last_slice)[:, None, None], centre - padded[2:, 1:-1], 0.0)
    upper = jnp.where((row_index > 0)[None, :, None], centre - padded[1:-1, :-2], 0.0)
    lower = jnp.where((row_index < last_row)[None, :, None], centre - padded[1:-1, 2:], 0.0)
    return 2.0 * smooth_weight * (below + above + upper + lower)


def local(density_raw, colour_raw, target, slab_rank):
    slices_dev = density_raw.shape[0]
    rows_dev = density_raw.shape[1]
    width = density_raw.shape[2]
    depth_count = lax.axis_size("depth")
    slices_total = slices_dev * depth_count
    partial_value, saved = slab_terms(density_raw, colour_raw, optical_depth / slices_total)
    pixels = rows_dev * width
    stacked = partial_value.reshape(4, 1, pixels)
    target_flat = target.reshape(3, pixels)
    position = lax.axis_index("depth")
    received = lax.all_gather(stacked, "depth", axis=1, tiled=True)
    answers = composite(received, slab_rank, target_flat)
    mine = lax.dynamic_index_in_dim(answers, position, 1, keepdims=False)
    mine = mine.reshape(4, rows_dev, width)
    grad_density, grad_colour = slab_gradients(saved, mine[:3], mine[3], slices_total)
    grad_density = grad_density + smooth_rims(density_raw, slices_dev, rows_dev)
    return (grad_density, grad_colour)


def solution(mesh):
    placed = (P("depth", "rows", None), P(None, "depth", "rows", None), P(None, "rows", None), P())
    return jax.shard_map(
        local,
        mesh=mesh,
        in_specs=placed,
        out_specs=(P("depth", "rows", None), P(None, "depth", "rows", None)),
        check_vma=False,
    )
```

profile of v0, /device:TPU:0, one launch (start us, length us, event | category | flops | bytes accessed | tf_op | source)
XLA Modules:
  0.0 106.4 jit_solution(17140207208497940315)
XLA Ops:
  7.2 2.4 %fusion.16 = f32[32,16,1024]{2,1,0:T(8,128)S(1)} fusion(bf16[32,16,1024]{2,1,0:T(8,128)(2,1)} %param.4), kind=kLoop, calls=%fused_computation.28 | loop fusion | flops 4194304 | bytes 3145728 | tf_op jit(solution)/shard_map/mul | solution.py:40
  9.7 1.2 %copy.40 = f32[4,8,16,1024]{3,1,2,0:T(8,128)S(1)} copy(f32[4,8,16,1024]{3,2,1,0:T(8,128)S(1)} %bitcast.83) | data formatting | bytes 4194304
  10.9 1.2 %fusion = f32[16384,32]{0,1:T(8,128)S(1)} fusion(f32[32,16384]{1,0:T(8,128)S(1)} %bitcast.81), kind=kOutput, calls=%fused_computation.2 | convolution fusion | flops 201851904 | bytes 4194304 | tf_op jit(solution)/shard_map/ij,cjp->cip/dot_general | solution.py:26
  12.1 1.2 %copy.41 = f32[4,8,16,1024]{3,2,1,0:T(8,128)S(1)} copy(f32[4,8,16,1024]{3,1,2,0:T(8,128)S(1)} %bitcast.82) | data formatting | bytes 4194304
  13.4 3.5 %bitcast_multiply_fusion = (f32[32,16,1024]{2,1,0:T(8,128)}, f32[32,16,1024]{2,1,0:T(8,128)S(1)}, f32[16,1024]{1,0:T(8,128)S(1)}) fusion(f32[4,8,16,1024]{3,2,1,0:T(8,128)S(1)} %copy.41, bf16[32,16,1024]{2,1,0:T(8,128)(2,1)S(1)} %copy-done.3), kind=kLoop, calls=%fused_computation.29 | loop fusion | flops 6799360 | bytes 7405568 | tf_op jit(solution)/shard_map/mul | solution.py:45
  16.8 3.6 %fusion.54 = (f32[3,16,1024]{2,1,0:T(8,128)S(1)}, f32[3,32,16,1024]{3,2,1,0:T(8,128)}) fusion(bf16[3,32,16,1024]{3,2,1,0:T(8,128)(2,1)S(1)} %copy-done.5, f32[32,16,1024]{2,1,0:T(8,128)S(1)} %get-tuple-element.13), kind=kLoop, calls=%fused_computation.91 | loop fusion | flops 9388032 | bytes 11730944 | tf_op jit(solution)/shard_map/reduce_sum | solution.py:50
  20.7 0.8 pad_maximum_fusion
  21.5 4.9 %collective-permute-start = (bf16[1,16,1024]{2,1,0:T(8,128)(2,1)S(1)}, bf16[1,16,1024]{2,1,0:T(8,128)(2,1)S(1)}, u32[]{:S(2)}, u32[]{:S(2)}) collective-permute-start(bf16[1,16,1024]{2,1,0:T(8,128)(2,1)S(1)} %get-tuple-element.18), channel_id=1, source_target_pairs={{0,4},{4,8},{8,12},{12,16},{16,20},{20,24},{24,28},{1,5},{5,9},{9,... | collective-permute-start | bytes 98312 | tf_op jit(solution)/shard_map/ppermute | solution.py:17
  26.4 1.5 %collective-permute-start.1 = (bf16[1,16,1024]{2,1,0:T(8,128)(2,1)S(1)}, bf16[1,16,1024]{2,1,0:T(8,128)(2,1)S(1)}, u32[]{:S(2)}, u32[]{:S(2)}) collective-permute-start(bf16[1,16,1024]{2,1,0:T(8,128)(2,1)S(1)} %get-tuple-element.17), channel_id=1, source_target_pairs={{4,0},{8,4},{12,8},{16,12},{20,16},{24,20},{28,24},{5,1},{9,5},{13... | collective-permute-start | bytes 98312 | tf_op jit(solution)/shard_map/ppermute | solution.py:18
  27.9 7.2 %reshape.104 = f32[3,32,16384]{2,1,0:T(8,128)} reshape(f32[3,32,16,1024]{3,2,1,0:T(8,128)} %get-tuple-element.9) | data formatting | bytes 12582912 | tf_op jit(solution)/shard_map/reshape | solution.py:25
  35.1 8.7 %fusion.39 = f32[3,16384,32]{1,2,0:T(8,128)} fusion(f32[3,32,16384]{2,1,0:T(8,128)} %reshape.104), kind=kOutput, calls=%fused_computation.72 | convolution fusion | flops 603980800 | bytes 12582912 | tf_op jit(solution)/shard_map/ij,cjp->cip/dot_general | solution.py:26
  43.8 0.9 copy.42
  44.7 10.2 %copy.44 = f32[12,8,16,1024]{3,2,1,0:T(8,128)} copy(f32[12,8,16,1024]{3,1,2,0:T(8,128)} %bitcast.76) | data formatting | bytes 12582912
  55.2 1.5 %collective-permute-start.2 = (bf16[34,1,1024]{2,0,1:T(8,128)(2,1)S(1)}, bf16[34,1,1024]{2,0,1:T(8,128)(2,1)S(1)}, u32[]{:S(2)}, u32[]{:S(2)}) collective-permute-start(bf16[34,1,1024]{2,0,1:T(8,128)(2,1)S(1)} %copy.34), channel_id=1, source_target_pairs={{0,1},{1,2},{2,3},{4,5},{5,6},{6,7},{8,9},{9,10},{10,11},{12,13},{... | collective-permute-start | bytes 208904 | tf_op jit(solution)/shard_map/ppermute | solution.py:17
  56.7 1.5 %collective-permute-start.3 = (bf16[34,1,1024]{2,0,1:T(8,128)(2,1)S(1)}, bf16[34,1,1024]{2,0,1:T(8,128)(2,1)S(1)}, u32[]{:S(2)}, u32[]{:S(2)}) collective-permute-start(bf16[34,1,1024]{2,0,1:T(8,128)(2,1)S(1)} %copy.35), channel_id=1, source_target_pairs={{1,0},{2,1},{3,2},{5,4},{6,5},{7,6},{9,8},{10,9},{11,10},{13,12},{... | collective-permute-start | bytes 208904 | tf_op jit(solution)/shard_map/ppermute | solution.py:18
  58.4 3.1 %collective-permute-done.3 = bf16[34,1,1024]{2,0,1:T(8,128)(2,1)S(1)} collective-permute-done((bf16[34,1,1024]{2,0,1:T(8,128)(2,1)S(1)}, bf16[34,1,1024]{2,0,1:T(8,128)(2,1)S(1)}, u32[]{:S(2)}, u32[]{:S(2)}) %collective-permute-start.3) | collective-permute-done | bytes 69664 | tf_op jit(solution)/shard_map/ppermute | solution.py:18
  62.3 11.4 %all-gather.2.cloned.1.call-done = f32[4,8,16384]{2,0,1:T(4,128)} async-done(((f32[4,1,16384]{2,0,1:T(4,128)}), f32[4,8,16384]{2,0,1:T(4,128)}) %all-gather.2.cloned.1.call-update) | async-done | bytes 2097168 | tf_op jit(solution)/shard_map/all_gather | solution.py:109
  73.7 3.9 %convolution_bitcast_fusion = f32[4,8,16384]{2,1,0:T(8,128)S(1)} fusion(f32[4,8,16384]{2,0,1:T(4,128)} %all-gather.2.cloned.1.call-done, s32[8]{0:T(128)S(1)} %copy-done.11), kind=kOutput, calls=%fused_computation | convolution fusion | flops 50331712 | bytes 4194336 | tf_op jit(solution)/shard_map/sk,csl->ckl/dot_general | solution.py:71
  79.1 1.0 fusion.32
  80.2 1.1 %fusion.26 = f32[4,16384,8]{1,2,0:T(8,128)S(1)} fusion(f32[1,8,16384]{2,1,0:T(8,128)S(1)} %bitcast_multiply_fusion.3, f32[3,8,16384]{2,1,0:T(8,128)S(1)} %broadcast_multiply_fusion.1, s32[8]{0:T(128)S(1)} %copy-done.11), kind=kOutput, calls=%fused_computation.45 | convolution fusion | flops 50856000 | bytes 4194336 | tf_op jit(solution)/shard_map/sk,ckl->csl/dot_general | solution.py:81
  81.9 0.8 broadcast_multiply_fusion.2
  83.6 1.5 %mul.151 = f32[16,1024]{1,0:T(8,128)} reshape(f32[16384]{0:T(1024)} %dynamic-slice_reduce_fusion.1) | data formatting | bytes 131072 | tf_op jit(solution)/shard_map/mul | solution.py:60
  85.0 8.7 %subtract_multiply_fusion = (f32[3,32,16,1024]{3,2,1,0:T(8,128)}, f32[32,16,1024]{2,1,0:T(8,128)S(1)}) fusion(f32[3,16,1024]{2,1,0:T(8,128)S(1)} %get-tuple-element.6, f32[32,16,1024]{2,1,0:T(8,128)} %copy-done.2, bf16[3,32,16,1024]{3,2,1,0:T(8,128)(2,1)} %param.5, f32[32,16,1024]{2,1,0:T(8,128)} %get-tuple-element.12, f32[3,16,1024]{2,1,0:T(8,128)} %get-tuple-element.7, ...), kind=kLoop, calls=%fused_computation.10 | loop fusion | flops 18350080 | bytes 22413312 | tf_op jit(solution)/shard_map/mul | solution.py:57
  93.8 5.7 %fusion.11 = f32[32,16,1024]{2,1,0:T(8,128)} fusion(bf16[32,16,1024]{2,1,0:T(8,128)(2,1)S(1)} %copy-done.4, f32[4,8,16,1024]{3,2,1,0:T(8,128)S(1)} %copy-done.1, f32[34,18,1024]{2,1,0:T(8,128)S(1)} %maximum_convert_fusion, f32[32,16,1024]{2,1,0:T(8,128)S(1)} %get-tuple-element.11, f32[16,1024]{1,0:T(8,128)S(1)} %copy-done.9, f32[16,1024]{1,0:T(8,128)S(1)} %copy-done.8, ...), kind=kLoop, calls=%fused_computation.23 | loop fusion | flops 18350080 | bytes 17956960 | tf_op jit(solution)/shard_map/add | solution.py:114
  (52 shorter events, 4.7 us)
Async XLA Ops:
  7.2 66.5 %all-gather.2.cloned.1.call-start = ((), (), s32[]{:S(2)}) async-start(), calls=%async_computation | async-start | bytes 2359296 | tf_op jit(solution)/shard_map/all_gather | solution.py:109
  12.1 1.2 %copy-start.3 = (bf16[32,16,1024]{2,1,0:T(8,128)(2,1)S(1)}, bf16[32,16,1024]{2,1,0:T(8,128)(2,1)}, u32[]{:S(2)}) copy-start(bf16[32,16,1024]{2,1,0:T(8,128)(2,1)} %param.4) | copy-start | bytes 3145732
  13.3 3.5 %copy-start = (f32[4,8,16,1024]{3,2,1,0:T(8,128)}, f32[4,8,16,1024]{3,2,1,0:T(8,128)S(1)}, u32[]{:S(2)}) copy-start(f32[4,8,16,1024]{3,2,1,0:T(8,128)S(1)} %copy.41) | copy-start | bytes 6291460
  13.3 3.5 %copy-start.5 = (bf16[3,32,16,1024]{3,2,1,0:T(8,128)(2,1)S(1)}, bf16[3,32,16,1024]{3,2,1,0:T(8,128)(2,1)}, u32[]{:S(2)}) copy-start(bf16[3,32,16,1024]{3,2,1,0:T(8,128)(2,1)} %param.5) | copy-start | bytes 9437188
  16.8 3.6 %copy-start.2 = (f32[32,16,1024]{2,1,0:T(8,128)}, f32[32,16,1024]{2,1,0:T(8,128)S(1)}, u32[]{:S(2)}) copy-start(f32[32,16,1024]{2,1,0:T(8,128)S(1)} %get-tuple-element.13) | copy-start | bytes 6291460
  20.6 14.6 %copy-start.7 = (f32[16,1024]{1,0:T(8,128)}, f32[16,1024]{1,0:T(8,128)S(1)}, u32[]{:S(2)}) copy-start(f32[16,1024]{1,0:T(8,128)S(1)} %negate_exponential_fusion) | copy-start | bytes 196612
  21.5 33.3 %collective-permute-start = (bf16[1,16,1024]{2,1,0:T(8,128)(2,1)S(1)}, bf16[1,16,1024]{2,1,0:T(8,128)(2,1)S(1)}, u32[]{:S(2)}, u32[]{:S(2)}) collective-permute-start(bf16[1,16,1024]{2,1,0:T(8,128)(2,1)S(1)} %get-tuple-element.18), channel_id=1, source_target_pairs={{0,4},{4,8},{8,12},{12,16},{16,20},{20,24},{24,28},{1,5},{5,9},{9,... | collective-permute-start | bytes 98312 | tf_op jit(solution)/shard_map/ppermute | solution.py:17
  26.4 28.5 %collective-permute-start.1 = (bf16[1,16,1024]{2,1,0:T(8,128)(2,1)S(1)}, bf16[1,16,1024]{2,1,0:T(8,128)(2,1)S(1)}, u32[]{:S(2)}, u32[]{:S(2)}) collective-permute-start(bf16[1,16,1024]{2,1,0:T(8,128)(2,1)S(1)} %get-tuple-element.17), channel_id=1, source_target_pairs={{4,0},{8,4},{12,8},{16,12},{20,16},{24,20},{28,24},{5,1},{9,5},{13... | collective-permute-start | bytes 98312 | tf_op jit(solution)/shard_map/ppermute | solution.py:18
  35.1 8.7 %copy-start.10 = (f32[3,16,1024]{2,1,0:T(8,128)S(1)}, f32[3,16,1024]{2,1,0:T(8,128)}, u32[]{:S(2)}) copy-start(f32[3,16,1024]{2,1,0:T(8,128)} %param.6) | copy-start | bytes 589828
  55.2 3.0 %collective-permute-start.2 = (bf16[34,1,1024]{2,0,1:T(8,128)(2,1)S(1)}, bf16[34,1,1024]{2,0,1:T(8,128)(2,1)S(1)}, u32[]{:S(2)}, u32[]{:S(2)}) collective-permute-start(bf16[34,1,1024]{2,0,1:T(8,128)(2,1)S(1)} %copy.34), channel_id=1, source_target_pairs={{0,1},{1,2},{2,3},{4,5},{5,6},{6,7},{8,9},{9,10},{10,11},{12,13},{... | collective-permute-start | bytes 208904 | tf_op jit(solution)/shard_map/ppermute | solution.py:17
  56.7 4.8 %collective-permute-start.3 = (bf16[34,1,1024]{2,0,1:T(8,128)(2,1)S(1)}, bf16[34,1,1024]{2,0,1:T(8,128)(2,1)S(1)}, u32[]{:S(2)}, u32[]{:S(2)}) collective-permute-start(bf16[34,1,1024]{2,0,1:T(8,128)(2,1)S(1)} %copy.35), channel_id=1, source_target_pairs={{1,0},{2,1},{3,2},{5,4},{6,5},{7,6},{9,8},{10,9},{11,10},{13,12},{... | collective-permute-start | bytes 208904 | tf_op jit(solution)/shard_map/ppermute | solution.py:18
  61.6 12.1 %copy-start.11 = (s32[8]{0:T(128)S(1)}, s32[8]{0:T(128)}, u32[]{:S(2)}) copy-start(s32[8]{0:T(128)} %param.7) | copy-start | bytes 100
  78.0 1.0 copy-start.6
  85.0 8.8 %copy-start.1 = (f32[4,8,16,1024]{3,2,1,0:T(8,128)S(1)}, f32[4,8,16,1024]{3,2,1,0:T(8,128)}, u32[]{:S(2)}) copy-start(f32[4,8,16,1024]{3,2,1,0:T(8,128)} %copy-done) | copy-start | bytes 6291460
  85.0 8.8 %copy-start.4 = (bf16[32,16,1024]{2,1,0:T(8,128)(2,1)S(1)}, bf16[32,16,1024]{2,1,0:T(8,128)(2,1)}, u32[]{:S(2)}) copy-start(bf16[32,16,1024]{2,1,0:T(8,128)(2,1)} %param.4) | copy-start | bytes 3145732
  85.0 8.8 %copy-start.8 = (f32[16,1024]{1,0:T(8,128)S(1)}, f32[16,1024]{1,0:T(8,128)}, u32[]{:S(2)}) copy-start(f32[16,1024]{1,0:T(8,128)} %copy-done.7) | copy-start | bytes 196612
  85.0 8.8 %copy-start.9 = (f32[16,1024]{1,0:T(8,128)S(1)}, f32[16,1024]{1,0:T(8,128)}, u32[]{:S(2)}) copy-start(f32[16,1024]{1,0:T(8,128)} %mul.151) | copy-start | bytes 196612
Sparse Core Ops, SparseCore 0:
  21.7 51.9 all-gather.1
where the time goes:
time: 107 us; the launch traced here: 106 us
  other arithmetic  27.3 us (26%)
  local copies, waits for them, and re-layouts  24.6 us (23%)
  matrix products  16.3 us (15%)
  waiting for transfers between devices  14.5 us (14%)
  between operations  14.3 us (13%)
  starting transfers between devices  9.35 us (9%)
    unnamed x30, local copies, waits for them, and re-layouts  13.8 us
    all_gather x1, waiting for transfers between devices, local(): received = lax.all_gather(stacked, 'depth', axis=1, tiled=True)  11.4 us
    dot_general x4, matrix products, along_rays(): jnp.einsum('ij,cjp->cip', matrix, flat, precision=lax.Precision.HIGHEST)  11.3 us
    mul x2, other arithmetic, slab_gradients(): slices_total * scaled_residual[:, None] * lit[None] * colour  9.56 us
    reshape x1, local copies, waits for them, and re-layouts, along_rays(): flat = values.reshape(shape[0], shape[1], -1)  7.22 us
    ppermute x2, starting transfers between devices, extended(): before = lax.ppermute(last, axis, up)  6.32 us
    add x1, other arithmetic, local(): grad_density = grad_density + smooth_rims(density_raw, slices_dev, rows_dev)  5.7 us
    dot_general x1, matrix products, composite(): jnp.einsum('sk,csl->ckl', one_hot, partials, precision=lax.Precision.HIGH...  3.86 us
  transfers between devices with their start and end apart: 5, of which 2 were waited for; matrix products, arithmetic and copies ran while one was open for 27% of the time, Pallas kernels for 0%

commit v1 on v0

--- a/solution.py
+++ b/solution.py
@@ -5,6 +5,28 @@
 
 optical_depth = 2.5
 smooth_weight = 0.05
+
+
+def laid_out(tiles, dim):
+    tiles = jnp.moveaxis(tiles, 0, dim)
+    lengths = tiles.shape
+    return tiles.reshape(*lengths[:dim], lengths[dim] * lengths[dim + 1], *lengths[dim + 2 :])
+
+
+def gather_around(array, axis, dim):
+    length = lax.axis_size(axis)
+    pairs = [(i, (i + 1) % length) for i in range(length)]
+    back = [(b, a) for a, b in pairs]
+    lower, upper = ([], [])
+    for step in range(length - 1):
+        if step % 2 == 0:
+            lower.append(lax.ppermute(lower[-1] if lower else array, axis, pairs))
+        else:
+            upper.append(lax.ppermute(upper[-1] if upper else array, axis, back))
+    blocks = jnp.stack([*lower[::-1], array, *upper])
+    shift = lax.axis_index(axis) - len(lower)
+    blocks = blocks[(jnp.arange(length) - shift) % length]
+    return laid_out(blocks, dim)
 
 
 def extended(value, sides, width):
@@ -106,7 +128,7 @@
     stacked = partial_value.reshape(4, 1, pixels)
     target_flat = target.reshape(3, pixels)
     position = lax.axis_index("depth")
-    received = lax.all_gather(stacked, "depth", axis=1, tiled=True)
+    received = gather_around(stacked, "depth", 1)
     answers = composite(received, slab_rank, target_flat)
     mine = lax.dynamic_index_in_dim(answers, position, 1, keepdims=False)
     mine = mine.reshape(4, rows_dev, width)

time: 107 us -> 115 us (1.075)
  the two profiles are of different devices: /device:TPU:0 before, /device:TPU:29 now
where the time goes in v1:
time: 115 us; the launch traced here: 114 us
  local copies, waits for them, and re-layouts  34 us (30%)
  other arithmetic  27.5 us (24%)
  starting transfers between devices  22 us (19%)
  matrix products  16.3 us (14%)
  waiting for transfers between devices  13.5 us (12%)
    unnamed x40, local copies, waits for them, and re-layouts  19.1 us
    dot_general x4, matrix products, along_rays(): jnp.einsum('ij,cjp->cip', matrix, flat, precision=lax.Precision.HIGHEST)  11.3 us
    mul x2, other arithmetic, slab_gradients(): slices_total * scaled_residual[:, None] * lit[None] * colour  9.71 us
    ppermute x4, waiting for transfers between devices, gather_around(): lower.append(lax.ppermute(lower[-1] if lower else array, axis, pairs))  7.62 us
    reshape x1, local copies, waits for them, and re-layouts, along_rays(): flat = values.reshape(shape[0], shape[1], -1)  7.16 us
    ppermute x4, starting transfers between devices, gather_around(): lower.append(lax.ppermute(lower[-1] if lower else array, axis, pairs))  6.46 us
    ppermute x2, starting transfers between devices, extended(): before = lax.ppermute(last, axis, up)  6.18 us
    ppermute x2, starting transfers between devices, extended(): after = lax.ppermute(initial, axis, down)  6.09 us
  transfers between devices with their start and end apart: 11, of which 2 were waited for; matrix products, arithmetic and copies ran while one was open for 31% of the time, Pallas kernels for 0%

profile of v1, /device:TPU:29, one launch (start us, length us, event | category | flops | bytes accessed | tf_op | source)
XLA Modules:
  0.0 114.4 jit_solution(11903025750716542802)
XLA Ops:
  0.6 2.4 %fusion.16 = f32[32,16,1024]{2,1,0:T(8,128)S(1)} fusion(bf16[32,16,1024]{2,1,0:T(8,128)(2,1)} %param.4), kind=kLoop, calls=%fused_computation.29 | loop fusion | flops 4194304 | bytes 3145728 | tf_op jit(solution)/shard_map/mul | solution.py:62
  3.1 1.2 %copy.72 = f32[4,8,16,1024]{3,1,2,0:T(8,128)S(1)} copy(f32[4,8,16,1024]{3,2,1,0:T(8,128)S(1)} %bitcast.119) | data formatting | bytes 4194304
  4.3 1.2 %fusion = f32[16384,32]{0,1:T(8,128)S(1)} fusion(f32[32,16384]{1,0:T(8,128)S(1)} %bitcast.117), kind=kOutput, calls=%fused_computation.3 | convolution fusion | flops 201851904 | bytes 4194304 | tf_op jit(solution)/shard_map/ij,cjp->cip/dot_general | solution.py:48
  5.5 1.2 %copy.73 = f32[4,8,16,1024]{3,2,1,0:T(8,128)S(1)} copy(f32[4,8,16,1024]{3,1,2,0:T(8,128)S(1)} %bitcast.118) | data formatting | bytes 4194304
  6.8 3.5 %bitcast_multiply_fusion = (f32[32,16,1024]{2,1,0:T(8,128)}, f32[32,16,1024]{2,1,0:T(8,128)S(1)}, f32[16,1024]{1,0:T(8,128)S(1)}) fusion(f32[4,8,16,1024]{3,2,1,0:T(8,128)S(1)} %copy.73, bf16[32,16,1024]{2,1,0:T(8,128)(2,1)S(1)} %copy-done.3), kind=kLoop, calls=%fused_computation.30 | loop fusion | flops 6799360 | bytes 7405568 | tf_op jit(solution)/shard_map/mul | solution.py:67
  10.2 3.6 %fusion.56 = (f32[3,16,1024]{2,1,0:T(8,128)S(1)}, f32[3,32,16,1024]{3,2,1,0:T(8,128)}) fusion(bf16[3,32,16,1024]{3,2,1,0:T(8,128)(2,1)S(1)} %copy-done.5, f32[32,16,1024]{2,1,0:T(8,128)S(1)} %get-tuple-element.13), kind=kLoop, calls=%fused_computation.107 | loop fusion | flops 9388032 | bytes 11730944 | tf_op jit(solution)/shard_map/reduce_sum | solution.py:72
  14.3 1.5 %collective-permute-start.4 = (f32[4,1,16384]{2,0,1:T(4,128)S(1)}, f32[4,1,16384]{2,0,1:T(4,128)}, u32[]{:S(2)}, u32[]{:S(2)}) collective-permute-start(f32[4,1,16384]{2,0,1:T(4,128)S(1)} %pad_maximum_fusion), channel_id=1, source_target_pairs={{4,0},{8,4},{12,8},{16,12},{20,16},{24,20},{28,24},{0,28},{5,1},{9... | collective-permute-start | bytes 786440 | tf_op jit(solution)/shard_map/ppermute | solution.py:25
  15.7 1.3 %collective-permute-start.7 = (bf16[1,16,1024]{2,1,0:T(8,128)(2,1)S(1)}, bf16[1,16,1024]{2,1,0:T(8,128)(2,1)S(1)}, u32[]{:S(2)}, u32[]{:S(2)}) collective-permute-start(bf16[1,16,1024]{2,1,0:T(8,128)(2,1)S(1)} %get-tuple-element.18), channel_id=1, source_target_pairs={{0,4},{4,8},{8,12},{12,16},{16,20},{20,24},{24,28},{1,5},{5,9},{9,... | collective-permute-start | bytes 98312 | tf_op jit(solution)/shard_map/ppermute | solution.py:39
  17.0 4.2 %collective-permute-start.8 = (bf16[1,16,1024]{2,1,0:T(8,128)(2,1)S(1)}, bf16[1,16,1024]{2,1,0:T(8,128)(2,1)S(1)}, u32[]{:S(2)}, u32[]{:S(2)}) collective-permute-start(bf16[1,16,1024]{2,1,0:T(8,128)(2,1)S(1)} %get-tuple-element.17), channel_id=1, source_target_pairs={{4,0},{8,4},{12,8},{16,12},{20,16},{24,20},{28,24},{5,1},{9,5},{13... | collective-permute-start | bytes 98312 | tf_op jit(solution)/shard_map/ppermute | solution.py:40
  21.2 7.2 %reshape.174 = f32[3,32,16384]{2,1,0:T(8,128)} reshape(f32[3,32,16,1024]{3,2,1,0:T(8,128)} %get-tuple-element.9) | data formatting | bytes 12582912 | tf_op jit(solution)/shard_map/reshape | solution.py:47
  28.4 8.6 %fusion.39 = f32[3,16384,32]{1,2,0:T(8,128)} fusion(f32[3,32,16384]{2,1,0:T(8,128)} %reshape.174), kind=kOutput, calls=%fused_computation.84 | convolution fusion | flops 603980800 | bytes 12582912 | tf_op jit(solution)/shard_map/ij,cjp->cip/dot_general | solution.py:48
  39.0 10.2 %copy.76 = f32[12,8,16,1024]{3,2,1,0:T(8,128)} copy(f32[12,8,16,1024]{3,1,2,0:T(8,128)} %bitcast.111) | data formatting | bytes 12582912
  49.2 2.1 %collective-permute-start.2 = (f32[4,1,16384]{2,0,1:T(4,128)S(1)}, f32[4,1,16384]{2,0,1:T(4,128)S(1)}, u32[]{:S(2)}, u32[]{:S(2)}) collective-permute-start(f32[4,1,16384]{2,0,1:T(4,128)S(1)} %collective-permute-done.1), channel_id=1, source_target_pairs={{0,4},{4,8},{8,12},{12,16},{16,20},{20,24},{24,28},{28,0},{1,5},{5... | collective-permute-start | bytes 786440 | tf_op jit(solution)/shard_map/ppermute | solution.py:23
  51.6 4.9 %collective-permute-start.9 = (bf16[34,1,1024]{2,0,1:T(8,128)(2,1)S(1)}, bf16[34,1,1024]{2,0,1:T(8,128)(2,1)S(1)}, u32[]{:S(2)}, u32[]{:S(2)}) collective-permute-start(bf16[34,1,1024]{2,0,1:T(8,128)(2,1)S(1)} %copy.66), channel_id=1, source_target_pairs={{0,1},{1,2},{2,3},{4,5},{5,6},{6,7},{8,9},{9,10},{10,11},{12,13},{... | collective-permute-start | bytes 208904 | tf_op jit(solution)/shard_map/ppermute | solution.py:39
  56.6 1.9 %collective-permute-start.10 = (bf16[34,1,1024]{2,0,1:T(8,128)(2,1)S(1)}, bf16[34,1,1024]{2,0,1:T(8,128)(2,1)S(1)}, u32[]{:S(2)}, u32[]{:S(2)}) collective-permute-start(bf16[34,1,1024]{2,0,1:T(8,128)(2,1)S(1)} %copy.67), channel_id=1, source_target_pairs={{1,0},{2,1},{3,2},{5,4},{6,5},{7,6},{9,8},{10,9},{11,10},{13,12},{... | collective-permute-start | bytes 208904 | tf_op jit(solution)/shard_map/ppermute | solution.py:40
  58.6 4.1 %collective-permute-start.3 = (f32[4,1,16384]{2,0,1:T(4,128)S(1)}, f32[4,1,16384]{2,0,1:T(4,128)S(1)}, u32[]{:S(2)}, u32[]{:S(2)}) collective-permute-start(f32[4,1,16384]{2,0,1:T(4,128)S(1)} %collective-permute-done.2), channel_id=1, source_target_pairs={{0,4},{4,8},{8,12},{12,16},{16,20},{20,24},{24,28},{28,0},{1,5},{5... | collective-permute-start | bytes 786440 | tf_op jit(solution)/shard_map/ppermute | solution.py:23
  63.8 5.9 %collective-permute-done.5 = f32[4,1,16384]{2,0,1:T(4,128)S(1)} collective-permute-done((f32[4,1,16384]{2,0,1:T(4,128)}, f32[4,1,16384]{2,0,1:T(4,128)S(1)}, u32[]{:S(2)}, u32[]{:S(2)}) %collective-permute-start.5) | collective-permute-done | bytes 262176 | tf_op jit(solution)/shard_map/ppermute | solution.py:25
  69.6 1.8 %collective-permute-start.6 = (f32[4,1,16384]{2,0,1:T(4,128)S(1)}, f32[4,1,16384]{2,0,1:T(4,128)S(1)}, u32[]{:S(2)}, u32[]{:S(2)}) collective-permute-start(f32[4,1,16384]{2,0,1:T(4,128)S(1)} %collective-permute-done.5), channel_id=1, source_target_pairs={{4,0},{8,4},{12,8},{16,12},{20,16},{24,20},{28,24},{0,28},{5,1},{9... | collective-permute-start | bytes 786440 | tf_op jit(solution)/shard_map/ppermute | solution.py:25
  71.4 7.6 %collective-permute-done.3 = f32[4,1,16384]{2,0,1:T(4,128)S(1)} collective-permute-done((f32[4,1,16384]{2,0,1:T(4,128)S(1)}, f32[4,1,16384]{2,0,1:T(4,128)S(1)}, u32[]{:S(2)}, u32[]{:S(2)}) %collective-permute-start.3) | collective-permute-done | bytes 262176 | tf_op jit(solution)/shard_map/ppermute | solution.py:23
  82.8 1.7 %bitcast_dynamic-update-slice_fusion.1 = f32[8,4,1,16384]{3,1,0,2:T(4,128)} fusion(f32[8,4,1,16384]{3,1,0,2:T(4,128)} %maximum_dynamic-update-slice_fusion, f32[4,1,16384]{2,0,1:T(4,128)} %collective-permute-done.4), kind=kLoop, calls=%fused_computation.67 | loop fusion | bytes 524288
  85.9 4.6 %gather_fusion = f32[8,4,16384]{2,1,0:T(4,128)} fusion(f32[8,4,16384]{2,1,0:T(4,128)} %bitcast.16, s32[1024]{0:T(1024)S(1)} %pad_clamp_fusion), kind=kCustom, calls=%fused_computation | custom fusion | bytes 4194336 | tf_op jit(solution)/shard_map/gather | solution.py:28
  90.5 3.9 %convolution_bitcast_fusion = f32[4,8,16384]{2,1,0:T(8,128)S(1)} fusion(f32[4,8,16384]{2,0,1:T(4,128)} %bitcast.116, s32[8]{0:T(128)S(1)} %copy-done.13), kind=kOutput, calls=%fused_computation.1 | convolution fusion | flops 50331712 | bytes 4194336 | tf_op jit(solution)/shard_map/sk,csl->ckl/dot_general | solution.py:93
  99.8 8.8 %subtract_multiply_fusion = (f32[3,32,16,1024]{3,2,1,0:T(8,128)}, f32[32,16,1024]{2,1,0:T(8,128)S(1)}) fusion(f32[3,16,1024]{2,1,0:T(8,128)} %get-tuple-element.6, f32[32,16,1024]{2,1,0:T(8,128)} %copy-done.2, bf16[3,32,16,1024]{3,2,1,0:T(8,128)(2,1)} %param.5, f32[32,16,1024]{2,1,0:T(8,128)} %get-tuple-element.12, f32[3,16,1024]{2,1,0:T(8,128)} %get-tuple-element.7, ...), kind=kLoop, calls=%fused_computation.11 | loop fusion | flops 18350080 | bytes 22413312 | tf_op jit(solution)/shard_map/mul | solution.py:79
  108.7 5.7 %fusion.11 = f32[32,16,1024]{2,1,0:T(8,128)} fusion(bf16[32,16,1024]{2,1,0:T(8,128)(2,1)S(1)} %copy-done.4, f32[4,8,16,1024]{3,2,1,0:T(8,128)S(1)} %copy-done.1, f32[34,18,1024]{2,1,0:T(8,128)S(1)} %maximum_convert_fusion, f32[32,16,1024]{2,1,0:T(8,128)S(1)} %get-tuple-element.11, f32[16,1024]{1,0:T(8,128)S(1)} %mul.151, ...), kind=kLoop, calls=%fused_computation.24 | loop fusion | flops 18350080 | bytes 17956960 | tf_op jit(solution)/shard_map/add | solution.py:136
  (80 shorter events, 14.3 us)
Async XLA Ops:
  5.5 1.2 %copy-start.3 = (bf16[32,16,1024]{2,1,0:T(8,128)(2,1)S(1)}, bf16[32,16,1024]{2,1,0:T(8,128)(2,1)}, u32[]{:S(2)}) copy-start(bf16[32,16,1024]{2,1,0:T(8,128)(2,1)} %param.4) | copy-start | bytes 3145732
  6.8 3.5 %copy-start = (f32[4,8,16,1024]{3,2,1,0:T(8,128)}, f32[4,8,16,1024]{3,2,1,0:T(8,128)S(1)}, u32[]{:S(2)}) copy-start(f32[4,8,16,1024]{3,2,1,0:T(8,128)S(1)} %copy.73) | copy-start | bytes 6291460
  6.8 3.5 %copy-start.5 = (bf16[3,32,16,1024]{3,2,1,0:T(8,128)(2,1)S(1)}, bf16[3,32,16,1024]{3,2,1,0:T(8,128)(2,1)}, u32[]{:S(2)}) copy-start(bf16[3,32,16,1024]{3,2,1,0:T(8,128)(2,1)} %param.5) | copy-start | bytes 9437188
  10.2 3.6 %copy-start.2 = (f32[32,16,1024]{2,1,0:T(8,128)}, f32[32,16,1024]{2,1,0:T(8,128)S(1)}, u32[]{:S(2)}) copy-start(f32[32,16,1024]{2,1,0:T(8,128)S(1)} %get-tuple-element.13) | copy-start | bytes 6291460
  14.2 22.8 %collective-permute-start = (f32[4,1,16384]{2,0,1:T(4,128)S(1)}, f32[4,1,16384]{2,0,1:T(4,128)S(1)}, u32[]{:S(2)}, u32[]{:S(2)}) collective-permute-start(f32[4,1,16384]{2,0,1:T(4,128)S(1)} %pad_maximum_fusion), channel_id=1, source_target_pairs={{0,4},{4,8},{8,12},{12,16},{16,20},{20,24},{24,28},{28,0},{1,5},{5... | collective-permute-start | bytes 786440 | tf_op jit(solution)/shard_map/ppermute | solution.py:23
  14.3 44.2 %collective-permute-start.4 = (f32[4,1,16384]{2,0,1:T(4,128)S(1)}, f32[4,1,16384]{2,0,1:T(4,128)}, u32[]{:S(2)}, u32[]{:S(2)}) collective-permute-start(f32[4,1,16384]{2,0,1:T(4,128)S(1)} %pad_maximum_fusion), channel_id=1, source_target_pairs={{4,0},{8,4},{12,8},{16,12},{20,16},{24,20},{28,24},{0,28},{5,1},{9... | collective-permute-start | bytes 786440 | tf_op jit(solution)/shard_map/ppermute | solution.py:25
  15.7 33.4 %collective-permute-start.7 = (bf16[1,16,1024]{2,1,0:T(8,128)(2,1)S(1)}, bf16[1,16,1024]{2,1,0:T(8,128)(2,1)S(1)}, u32[]{:S(2)}, u32[]{:S(2)}) collective-permute-start(bf16[1,16,1024]{2,1,0:T(8,128)(2,1)S(1)} %get-tuple-element.18), channel_id=1, source_target_pairs={{0,4},{4,8},{8,12},{12,16},{16,20},{20,24},{24,28},{1,5},{5,9},{9,... | collective-permute-start | bytes 98312 | tf_op jit(solution)/shard_map/ppermute | solution.py:39
  17.0 34.3 %collective-permute-start.8 = (bf16[1,16,1024]{2,1,0:T(8,128)(2,1)S(1)}, bf16[1,16,1024]{2,1,0:T(8,128)(2,1)S(1)}, u32[]{:S(2)}, u32[]{:S(2)}) collective-permute-start(bf16[1,16,1024]{2,1,0:T(8,128)(2,1)S(1)} %get-tuple-element.17), channel_id=1, source_target_pairs={{4,0},{8,4},{12,8},{16,12},{20,16},{24,20},{28,24},{5,1},{9,5},{13... | collective-permute-start | bytes 98312 | tf_op jit(solution)/shard_map/ppermute | solution.py:40
  28.3 9.8 %copy-start.12 = (f32[3,16,1024]{2,1,0:T(8,128)S(1)}, f32[3,16,1024]{2,1,0:T(8,128)}, u32[]{:S(2)}) copy-start(f32[3,16,1024]{2,1,0:T(8,128)} %param.6) | copy-start | bytes 589828
  37.0 12.1 %copy-start.8 = (f32[4,1,16384]{2,0,1:T(4,128)}, f32[4,1,16384]{2,0,1:T(4,128)S(1)}, u32[]{:S(2)}) copy-start(f32[4,1,16384]{2,0,1:T(4,128)S(1)} %collective-permute-done) | copy-start | bytes 786436
  37.0 12.2 %collective-permute-start.1 = (f32[4,1,16384]{2,0,1:T(4,128)S(1)}, f32[4,1,16384]{2,0,1:T(4,128)S(1)}, u32[]{:S(2)}, u32[]{:S(2)}) collective-permute-start(f32[4,1,16384]{2,0,1:T(4,128)S(1)} %collective-permute-done), channel_id=1, source_target_pairs={{0,4},{4,8},{8,12},{12,16},{16,20},{20,24},{24,28},{28,0},{1,5},{5... | collective-permute-start | bytes 786440 | tf_op jit(solution)/shard_map/ppermute | solution.py:23
  49.2 13.7 %copy-start.10 = (f32[4,1,16384]{2,0,1:T(4,128)}, f32[4,1,16384]{2,0,1:T(4,128)S(1)}, u32[]{:S(2)}) copy-start(f32[4,1,16384]{2,0,1:T(4,128)S(1)} %collective-permute-done.1) | copy-start | bytes 786436
  49.2 9.4 %collective-permute-start.2 = (f32[4,1,16384]{2,0,1:T(4,128)S(1)}, f32[4,1,16384]{2,0,1:T(4,128)S(1)}, u32[]{:S(2)}, u32[]{:S(2)}) collective-permute-start(f32[4,1,16384]{2,0,1:T(4,128)S(1)} %collective-permute-done.1), channel_id=1, source_target_pairs={{0,4},{4,8},{8,12},{12,16},{16,20},{20,24},{24,28},{28,0},{1,5},{5... | collective-permute-start | bytes 786440 | tf_op jit(solution)/shard_map/ppermute | solution.py:23
  51.6 11.1 %collective-permute-start.9 = (bf16[34,1,1024]{2,0,1:T(8,128)(2,1)S(1)}, bf16[34,1,1024]{2,0,1:T(8,128)(2,1)S(1)}, u32[]{:S(2)}, u32[]{:S(2)}) collective-permute-start(bf16[34,1,1024]{2,0,1:T(8,128)(2,1)S(1)} %copy.66), channel_id=1, source_target_pairs={{0,1},{1,2},{2,3},{4,5},{5,6},{6,7},{8,9},{9,10},{10,11},{12,13},{... | collective-permute-start | bytes 208904 | tf_op jit(solution)/shard_map/ppermute | solution.py:39
  56.6 6.3 %collective-permute-start.10 = (bf16[34,1,1024]{2,0,1:T(8,128)(2,1)S(1)}, bf16[34,1,1024]{2,0,1:T(8,128)(2,1)S(1)}, u32[]{:S(2)}, u32[]{:S(2)}) collective-permute-start(bf16[34,1,1024]{2,0,1:T(8,128)(2,1)S(1)} %copy.67), channel_id=1, source_target_pairs={{1,0},{2,1},{3,2},{5,4},{6,5},{7,6},{9,8},{10,9},{11,10},{13,12},{... | collective-permute-start | bytes 208904 | tf_op jit(solution)/shard_map/ppermute | solution.py:40
  58.5 11.1 %collective-permute-start.5 = (f32[4,1,16384]{2,0,1:T(4,128)}, f32[4,1,16384]{2,0,1:T(4,128)S(1)}, u32[]{:S(2)}, u32[]{:S(2)}) collective-permute-start(f32[4,1,16384]{2,0,1:T(4,128)} %collective-permute-done.4), channel_id=1, source_target_pairs={{4,0},{8,4},{12,8},{16,12},{20,16},{24,20},{28,24},{0,28},{5,1},{9... | collective-permute-start | bytes 786440 | tf_op jit(solution)/shard_map/ppermute | solution.py:25
  58.6 20.5 %collective-permute-start.3 = (f32[4,1,16384]{2,0,1:T(4,128)S(1)}, f32[4,1,16384]{2,0,1:T(4,128)S(1)}, u32[]{:S(2)}, u32[]{:S(2)}) collective-permute-start(f32[4,1,16384]{2,0,1:T(4,128)S(1)} %collective-permute-done.2), channel_id=1, source_target_pairs={{0,4},{4,8},{8,12},{12,16},{16,20},{20,24},{24,28},{28,0},{1,5},{5... | collective-permute-start | bytes 786440 | tf_op jit(solution)/shard_map/ppermute | solution.py:23
  63.0 17.5 %copy-start.11 = (f32[4,1,16384]{2,0,1:T(4,128)S(1)}, f32[4,1,16384]{2,0,1:T(4,128)}, u32[]{:S(2)}) copy-start(f32[4,1,16384]{2,0,1:T(4,128)} %copy-done.10) | copy-start | bytes 786436
  63.0 18.2 %copy-start.9 = (f32[4,1,16384]{2,0,1:T(4,128)S(1)}, f32[4,1,16384]{2,0,1:T(4,128)}, u32[]{:S(2)}) copy-start(f32[4,1,16384]{2,0,1:T(4,128)} %copy-done.8) | copy-start | bytes 786436
  63.8 18.2 %copy-start.7 = (f32[1,3,1,16384]{3,1,2,0:T(4,128)S(1)}, f32[1,3,1,16384]{3,1,2,0:T(4,128)}, u32[]{:S(2)}) copy-start(f32[1,3,1,16384]{3,1,2,0:T(4,128)} %concatenate.22) | copy-start | bytes 589828
  69.6 15.5 %collective-permute-start.6 = (f32[4,1,16384]{2,0,1:T(4,128)S(1)}, f32[4,1,16384]{2,0,1:T(4,128)S(1)}, u32[]{:S(2)}, u32[]{:S(2)}) collective-permute-start(f32[4,1,16384]{2,0,1:T(4,128)S(1)} %collective-permute-done.5), channel_id=1, source_target_pairs={{4,0},{8,4},{12,8},{16,12},{20,16},{24,20},{28,24},{0,28},{5,1},{9... | collective-permute-start | bytes 786440 | tf_op jit(solution)/shard_map/ppermute | solution.py:25
  85.9 4.6 %copy-start.13 = (s32[8]{0:T(128)S(1)}, s32[8]{0:T(128)}, u32[]{:S(2)}) copy-start(s32[8]{0:T(128)} %param.7) | copy-start | bytes 100
  99.8 8.8 %copy-start.1 = (f32[4,8,16,1024]{3,2,1,0:T(8,128)S(1)}, f32[4,8,16,1024]{3,2,1,0:T(8,128)}, u32[]{:S(2)}) copy-start(f32[4,8,16,1024]{3,2,1,0:T(8,128)} %copy-done) | copy-start | bytes 6291460
  99.8 8.8 %copy-start.4 = (bf16[32,16,1024]{2,1,0:T(8,128)(2,1)S(1)}, bf16[32,16,1024]{2,1,0:T(8,128)(2,1)}, u32[]{:S(2)}) copy-start(bf16[32,16,1024]{2,1,0:T(8,128)(2,1)} %param.4) | copy-start | bytes 3145732
  (1 other events, 1.0 us)
